TPU v7x, 256 devices: a whole 4x4x8 slice. The times are simulated.
256 devices in a mesh: facet: 8 (over y_lo, x), vis: 16 (over z, core), spec: 2 (over y_hi).
Axes of the slice: x: 4, y: 4 (y_hi: 2, y_lo: 2; y = y_hi * 2 + y_lo), z: 8, core: 2. Of those that a mesh axis runs over, the one named last changes fastest.
Arguments:
- image: float32 [1024, 8, 4096], P(('facet', 'vis'), 'spec'), may hold values from 0 to 1
- wavelet_dual: float32 [1024, 8, 4096], P(('facet', 'vis'), 'spec'), may hold values from -6 to 6
- weights: float32 [1024, 4096], P(('facet', 'vis')), may hold values from 0.3 to 3
- kernels: bfloat16 [8, 16, 2, 256, 128], P('facet', 'vis'), may hold values from -0.375 to 0.375
- vis_data: bfloat16 [8, 16, 8, 2, 16, 256, 128], P('facet', 'vis', 'spec'), may hold values from -6 to 6
- tile_list: int32 [8, 16, 16], P('facet', 'vis'), may hold values from 0 to 31, as said below
- tile_count: int32 [8, 16], P('facet', 'vis'), may hold values from 4 to 16, as said below
Outputs:
- image_next: float32 [1024, 8, 4096], P(('facet', 'vis'), 'spec')
- dual_next: float32 [1024, 8, 4096], P(('facet', 'vis'), 'spec')
Inputs may be any that keep to these rules, and one draw needn't show every extreme that they name: `tile_list`: the 16 slots of a block name distinct tiles; slots from tile_count on are unused. `tile_count`: every draw has a block with 16 occupied slots and one with the fewest allowed.
All inputs are finite; a program needn't handle non-finite values.
Results may differ from a plain program's by a relative error of at most 0.017.
Values may be sent and summed in bfloat16 or wider, within the bound.
No kernel may reach another device: no remote copies, remote signals or barrier semaphores. Data moves between devices by JAX's collectives and lax.ppermute only.
A program may use at most 128 MiB of HBM per device.

v0:
```python
import math
import jax
import jax.numpy as jnp
from jax import lax
from jax.sharding import PartitionSpec as P

root_three = math.sqrt(3.0)
norm_factor = 4.0 * math.sqrt(2.0)
low_taps = [
    (1.0 + root_three) / norm_factor,
    (3.0 + root_three) / norm_factor,
    (3.0 - root_three) / norm_factor,
    (1.0 - root_three) / norm_factor,
]
high_taps = [low_taps[3], -low_taps[2], low_taps[1], -low_taps[0]]
primal_step = 0.2
dual_step = 0.5
tile_width = 128
highest = lax.Precision.HIGHEST


def shifted(value, axis, steps):
    count = lax.axis_size(axis)
    initial, last = (max(0, -steps), min(count, count - steps))
    return lax.ppermute(value, axis, [(source, source + steps) for source in range(initial, last)])


def for_sending(x):

    def short(part):
        return part.astype(jnp.bfloat16) if part.dtype == jnp.float32 else part

    return jax.tree.map(short, x)


def phase_table(rows_count, cols_count, modulus):
    rows_index = jnp.arange(rows_count, dtype=jnp.int32)
    cols_index = jnp.arange(cols_count, dtype=jnp.int32)
    angle = (rows_index[:, None] * cols_index[None, :] % modulus).astype(jnp.float32) * (
        2.0 * math.pi / modulus
    )
    return (jnp.cos(angle), jnp.sin(angle))


def across_outer(values, table):
    return jnp.einsum(
        "qab,ak->qkb", values, table, precision=highest, preferred_element_type=jnp.float32
    )


def along_inner(values, table):
    return jnp.einsum(
        "qkb,bj->qkj", values, table, precision=highest, preferred_element_type=jnp.float32
    )


def fourier_rows(real_part, imag_part, sign):
    rows_count, length = real_part.shape
    outer = length // tile_width
    cos_outer, sin_outer = phase_table(outer, outer, outer)
    cos_twist, sin_twist = phase_table(outer, tile_width, length)
    cos_inner, sin_inner = phase_table(tile_width, tile_width, tile_width)
    first_re = real_part.reshape(rows_count, outer, tile_width)
    first_im = imag_part.reshape(rows_count, outer, tile_width)
    section_re = across_outer(first_re, cos_outer) - sign * across_outer(first_im, sin_outer)
    section_im = across_outer(first_im, cos_outer) + sign * across_outer(first_re, sin_outer)
    twist_re = section_re * cos_twist - sign * section_im * sin_twist
    twist_im = section_im * cos_twist + sign * section_re * sin_twist
    final_re = along_inner(twist_re, cos_inner) - sign * along_inner(twist_im, sin_inner)
    final_im = along_inner(twist_im, cos_inner) + sign * along_inner(twist_re, sin_inner)
    unit_scale = 1.0 / math.sqrt(length)
    final_re = jnp.swapaxes(final_re, 1, 2).reshape(rows_count, length) * unit_scale
    final_im = jnp.swapaxes(final_im, 1, 2).reshape(rows_count, length) * unit_scale
    return (final_re, final_im)


def kernel_blocks(kernel_pair):
    real_k = kernel_pair[0]
    imag_k = kernel_pair[1]
    top_row = jnp.stack([real_k, -imag_k], axis=1)
    bottom_row = jnp.stack([imag_k, real_k], axis=1)
    return jnp.stack([top_row, bottom_row], axis=0)


def per_device(image, wavelet_dual, weights, kernels, vis_data, tile_list, tile_count):
    panel_rows, chan_count, grid_width = image.shape
    tiles_count = grid_width // tile_width
    stacked = kernel_blocks(kernels[0, 0])
    own_list = tile_list[0, 0]
    slots_count = own_list.shape[0]
    own_data = vis_data[0, 0]
    own_count = tile_count[0, 0]
    columns = jnp.arange(tiles_count, dtype=jnp.int32)
    one_hot = (own_list[:, None] == columns[None, :]).astype(jnp.bfloat16)
    image_rows = image.reshape(panel_rows * chan_count, grid_width)
    grid_re, grid_im = fourier_rows(image_rows, jnp.zeros_like(image_rows), -1.0)
    grid_panel = (
        jnp.stack([grid_re, grid_im], axis=1)
        .reshape(panel_rows, chan_count, 2, grid_width)
        .astype(jnp.bfloat16)
    )
    live_slots = (jnp.arange(slots_count, dtype=jnp.int32) < own_count)[None, None, :, None, None]
    shard_rows = lax.all_gather(grid_panel, "vis", axis=0, tiled=True)
    rows_here = shard_rows.shape[0]
    split_rows = shard_rows.reshape(rows_here, chan_count, 2, tiles_count, tile_width)
    picked = jnp.einsum(
        "rcitn,kt->rcikn", split_rows, one_hot, preferred_element_type=jnp.float32
    ).astype(jnp.bfloat16)
    kernel_rows = stacked
    predicted = jnp.einsum(
        "omir,rcikn->cokmn", kernel_rows, picked, preferred_element_type=jnp.float32
    )
    residual = jnp.where(live_slots, predicted - own_data.astype(jnp.float32), 0.0).astype(
        jnp.bfloat16
    )
    kernel_rows = stacked
    partial_tiles = jnp.einsum(
        "omir,cokmn->rcikn", kernel_rows, residual, preferred_element_type=jnp.float32
    ).astype(jnp.bfloat16)
    placed = jnp.einsum(
        "rcikn,kt->rcitn", partial_tiles, one_hot, preferred_element_type=jnp.float32
    )
    grid_sums = lax.psum_scatter(
        placed.reshape(lax.axis_size("vis") * panel_rows, chan_count, 2, grid_width).astype(
            jnp.bfloat16
        ),
        "vis",
        scatter_dimension=0,
        tiled=True,
    ).astype(jnp.float32)
    sums_rows = grid_sums.reshape(panel_rows * chan_count, 2, grid_width)
    grad_re, grad_im = fourier_rows(sums_rows[:, 0], sums_rows[:, 1], 1.0)
    gradient = grad_re.reshape(panel_rows, chan_count, grid_width)
    upper_rim = shifted(
        wavelet_dual[panel_rows - 3 :].astype(jnp.bfloat16), ("facet", "vis"), 1
    ).astype(jnp.float32)
    padded_dual = jnp.concatenate([upper_rim, wavelet_dual], axis=0)
    synthesized = jnp.zeros_like(wavelet_dual)
    for offset in range(4):
        synthesized = (
            synthesized + high_taps[offset] * padded_dual[3 - offset : 3 - offset + panel_rows]
        )
    image_next = jnp.maximum(image - primal_step * (gradient + synthesized), 0.0)
    extrap = 2.0 * image_next - image
    lower_rim = shifted(for_sending(extrap[:3]), ("facet", "vis"), -1)
    padded_next = jnp.concatenate([extrap, lower_rim], axis=0)
    detail = jnp.zeros_like(extrap)
    for offset in range(4):
        detail = detail + high_taps[offset] * padded_next[offset : offset + panel_rows]
    update = wavelet_dual + dual_step * detail
    energy = lax.psum(jnp.sum(update * update, axis=1).astype(jnp.bfloat16), "spec").astype(
        jnp.float32
    )
    dual_next = update * weights[:, None, :] / jnp.maximum(weights, jnp.sqrt(energy))[:, None, :]
    return (image_next, dual_next)


def solution(mesh):
    return jax.shard_map(
        per_device,
        mesh=mesh,
        in_specs=(
            P(("facet", "vis"), "spec", None),
            P(("facet", "vis"), "spec", None),
            P(("facet", "vis"), None),
            P("facet", "vis", None, None, None),
            P("facet", "vis", "spec", None, None, None, None),
            P("facet", "vis", None),
            P("facet", "vis"),
        ),
        out_specs=(P(("facet", "vis"), "spec", None), P(("facet", "vis"), "spec", None)),
        check_vma=False,
    )
```

profile of v0, /device:TPU:1, one launch (start us, length us, event | category | flops | bytes accessed | tf_op | source)
XLA Modules:
  0.0 359.4 jit_solution(1260190742002572805)
XLA Ops:
  7.7 1.4 reshape_reshape.3
  13.2 1.1 fusion.24
  15.8 1.1 fusion.23
  18.5 1.2 pad_maximum_fusion.2
  19.9 11.5 %copy.69 = bf16[1,1,4,2,16,256,128]{5,6,4,3,2,1,0:T(8,128)(2,1)} copy(bf16[1,1,4,2,16,256,128]{6,5,4,3,2,1,0:T(8,128)(2,1)} %param.11) | data formatting | bytes 16777216 | tf_op args[4]
  32.1 47.8 %all-gather.2.cloned.1.call-done = bf16[128,4,2,4096]{3,1,0,2:T(4,128)(2,1)} async-done(((bf16[8,4,2,4096]{3,1,0,2:T(4,128)(2,1)}), bf16[128,4,2,4096]{3,1,0,2:T(4,128)(2,1)}) %all-gather.2.cloned.1.call-update) | async-done | bytes 8388624 | tf_op jit(solution)/shard_map/all_gather | solution.py:103
  80.0 15.8 %reshape.128 = bf16[128,4,2,32,128]{4,3,1,0,2:T(8,128)(2,1)} reshape(bf16[128,4,2,4096]{3,1,0,2:T(4,128)(2,1)} %all-gather.2.cloned.1.call-done) | data formatting | bytes 16777216 | tf_op jit(solution)/shard_map/reshape | solution.py:105
  95.7 4.7 %convert_bitcast_fusion.1 = bf16[128,4,2,16,128,1]{4,3,2,1,0,5:T(8,128)(2,1)S(1)} fusion(bf16[128,4,2,32,128]{4,3,1,0,2:T(8,128)(2,1)} %reshape.128, s32[16]{0:T(128)S(1)} %bitcast.129), kind=kOutput, calls=%fused_computation.12 | convolution fusion | flops 136315392 | bytes 12582976 | tf_op jit(solution)/shard_map/rcitn,kt->rcikn/dot_general | solution.py:106
  100.4 15.2 %fusion.6 = bf16[4,2,16,256,128,1]{3,4,2,1,0,5:T(8,128)(2,1)} fusion(bf16[1,1,4,2,16,256,128]{5,6,4,3,2,1,0:T(8,128)(2,1)} %copy.69, pred[16]{0:T(512)(128)(4,1)S(1)} %iota_compare_fusion.1, bf16[128,4,2,16,128,1]{4,3,2,1,0,5:T(8,128)(2,1)S(1)} %convert_bitcast_fusion.1, bf16[1,256,2,128]{3,1,2,0:T(8,128)(2,1)S(1)} %get-tuple-element.15, ...), kind=kOutput, calls=%fused_computation.9 | convolution fusion | flops 2164785152 | bytes 21233680 | tf_op jit(solution)/shard_map/omir,rcikn->cokmn/dot_general | solution.py:110
  115.7 7.7 %fusion.7 = bf16[128,4,2,16,128]{0,4,2,3,1:T(8,128)(2,1)} fusion(bf16[4,2,16,256,128,1]{3,4,2,1,0,5:T(8,128)(2,1)} %fusion.6, bf16[1,256,2,128]{3,1,2,0:T(8,128)(2,1)S(1)} %get-tuple-element.15, bf16[1,256,2,128]{3,1,2,0:T(8,128)(2,1)S(1)} %get-tuple-element.14), kind=kOutput, calls=%fused_computation.10 | convolution fusion | flops 2149711872 | bytes 12845056 | tf_op jit(solution)/shard_map/omir,cokmn->rcikn/dot_general | solution.py:117
  123.4 8.0 %copy.72 = bf16[128,4,2,16,128]{4,3,2,1,0:T(8,128)(2,1)} copy(bf16[128,4,2,16,128]{0,4,2,3,1:T(8,128)(2,1)} %fusion.7) | data formatting | bytes 8388608 | tf_op jit(solution)/shard_map/convert_element_type | solution.py:119
  131.3 7.8 %convert_bitcast_fusion = bf16[128,4,2,32,128]{4,3,2,1,0:T(8,128)(2,1)} fusion(bf16[128,4,2,16,128]{4,3,2,1,0:T(8,128)(2,1)} %copy.72, s32[16]{0:T(128)S(1)} %bitcast.130), kind=kOutput, calls=%fused_computation.8 | convolution fusion | flops 138412544 | bytes 12582976 | tf_op jit(solution)/shard_map/rcikn,kt->rcitn/dot_general | solution.py:120
  139.2 12.5 %convert_element_type.116 = bf16[128,4,2,4096]{3,2,1,0:T(2,128)(2,1)} reshape(bf16[128,4,2,32,128]{4,3,2,1,0:T(8,128)(2,1)} %convert_bitcast_fusion) | data formatting | bytes 16777216 | tf_op jit(solution)/shard_map/convert_element_type | solution.py:124
  151.7 11.0 %copy.73 = bf16[128,4,2,4096]{3,1,2,0:T(4,128)(2,1)} copy(bf16[128,4,2,4096]{3,2,1,0:T(2,128)(2,1)} %convert_element_type.116) | data formatting | bytes 16777216 | tf_op jit(solution)/shard_map/convert_element_type | solution.py:124
  163.8 1.9 collective-permute-start
  167.4 127.4 %all-reduce.6.cloned.1.call-done = bf16[128,4,2,4096]{3,1,2,0:T(4,128)(2,1)} async-done(((bf16[128,4,2,4096]{3,1,2,0:T(4,128)(2,1)}), bf16[128,4,2,4096]{3,1,2,0:T(4,128)(2,1)}) %all-reduce.6.cloned.1.call-update) | async-done | bytes 8388624
  294.7 1.2 constant_dynamic-slice_fusion
  296.5 2.3 slice_reduce_fusion.1
  301.9 1.1 fusion.14
  304.6 2.4 multiply_subtract_fusion
  307.0 4.0 %collective-permute-start.1 = (bf16[3,4,4096]{2,1,0:T(4,128)(2,1)S(1)}, bf16[3,4,4096]{2,1,0:T(4,128)(2,1)S(1)}, u32[]{:S(2)}, u32[]{:S(2)}) collective-permute-start(bf16[3,4,4096]{2,1,0:T(4,128)(2,1)S(1)} %slice.138), channel_id=1, source_target_pairs={{2,0},{4,2},{6,4},{8,6},{10,8},{12,10},{14,12},{16,14},{18,16},{20... | collective-permute-start | bytes 294920 | tf_op jit(solution)/shard_map/ppermute | solution.py:25
  311.0 1.9 collective-permute-done.1
  313.0 1.3 multiply_reduce_fusion
  314.3 36.7 %all-reduce.4.cloned.1.call-done = bf16[8,4096]{1,0:T(8,128)(2,1)} async-done(((bf16[8,4096]{1,0:T(8,128)(2,1)}), bf16[8,4096]{1,0:T(8,128)(2,1)}) %all-reduce.4.cloned.1.call-update) | async-done | bytes 65552 | tf_op jit(solution)/shard_map/psum | solution.py:151
  (50 shorter events, 17.1 us)
Async XLA Ops:
  7.2 72.8 %all-gather.2.cloned.1.call-start = ((), (), s32[]{:S(2)}) async-start(), calls=%async_computation | async-start | bytes 8912896 | tf_op jit(solution)/shard_map/all_gather | solution.py:103
  19.7 12.4 %copy-start.2 = (bf16[1,1,2,256,128]{4,3,2,1,0:T(8,128)(2,1)S(1)}, bf16[1,1,2,256,128]{4,3,2,1,0:T(8,128)(2,1)}, u32[]{:S(2)}) copy-start(bf16[1,1,2,256,128]{4,3,2,1,0:T(8,128)(2,1)} %param.10) | copy-start | bytes 393220
  19.7 275.0 %all-reduce.6.cloned.1.call-start = ((), (), s32[]{:S(2)}) async-start(), calls=%async_computation.2 | async-start | bytes 16777216
  32.1 63.6 %copy-start.3 = (s32[1,1,16]{2,1,0:T(1,128)S(1)}, s32[1,1,16]{2,1,0:T(1,128)}, u32[]{:S(2)}) copy-start(s32[1,1,16]{2,1,0:T(1,128)} %param.12) | copy-start | bytes 196
  162.7 1.0 copy-start
  162.7 3.0 copy-start.4
  162.8 188.3 %all-reduce.4.cloned.1.call-start = ((), (), s32[]{:S(2)}) async-start(), calls=%async_computation.1 | async-start | bytes 131072 | tf_op jit(solution)/shard_map/psum | solution.py:151
  163.8 3.5 collective-permute-start
  299.8 51.3 %copy-start.1 = (f32[8,4096]{1,0:T(8,128)S(1)}, f32[8,4096]{1,0:T(8,128)}, u32[]{:S(2)}) copy-start(f32[8,4096]{1,0:T(8,128)} %param.9) | copy-start | bytes 393220
  307.0 5.9 %collective-permute-start.1 = (bf16[3,4,4096]{2,1,0:T(4,128)(2,1)S(1)}, bf16[3,4,4096]{2,1,0:T(4,128)(2,1)S(1)}, u32[]{:S(2)}, u32[]{:S(2)}) collective-permute-start(bf16[3,4,4096]{2,1,0:T(4,128)(2,1)S(1)} %slice.138), channel_id=1, source_target_pairs={{2,0},{4,2},{6,4},{8,6},{10,8},{12,10},{14,12},{16,14},{18,16},{20... | collective-permute-start | bytes 294920 | tf_op jit(solution)/shard_map/ppermute | solution.py:25
Sparse Core Ops, SparseCore 0:
  19.8 60.1 all-gather.1
  162.9 131.8 all-reduce.5
  314.4 36.5 all-reduce.3
where the time goes:
time: 361 us; the launch traced here: 359 us
  waiting for transfers between devices  214 us (59%)
  local copies, waits for them, and re-layouts  70.6 us (20%)
  matrix products  46.1 us (13%)
  between operations  15.3 us (4%)
  other arithmetic  7.01 us (2%)
  starting transfers between devices  6.25 us (2%)
    unnamed x4, waiting for transfers between devices  127 us
    all_gather x1, waiting for transfers between devices, per_device(): shard_rows = lax.all_gather(grid_panel, 'vis', axis=0, tiled=True)  47.8 us
    psum x1, waiting for transfers between devices, per_device(): lax.psum(jnp.sum(update * update, axis=1).astype(jnp.bfloat16), 'spec')  36.7 us
    convert_element_type x2, local copies, waits for them, and re-layouts, per_device(): placed.reshape(lax.axis_size('vis') * panel_rows, chan_count, 2, grid_width)  23.6 us
    reshape x1, local copies, waits for them, and re-layouts, per_device(): shard_rows.reshape(rows_here, chan_count, 2, tiles_count, tile_width)  15.8 us
    dot_general x1, matrix products, per_device(): jnp.einsum('omir,rcikn->cokmn', kernel_rows, picked, preferred_element_ty...  15.2 us
    unnamed x15, local copies, waits for them, and re-layouts  14.3 us
    convert_element_type x1, local copies, waits for them, and re-layouts, per_device(): partial_tiles = jnp.einsum('omir,cokmn->rcikn', kernel_rows, residual, pr...  7.97 us
  transfers between devices with their start and end apart: 5, of which 5 were waited for; matrix products, arithmetic and copies ran while one was open for 3% of the time, Pallas kernels for 0%

commit v1 on v0

--- a/solution.py
+++ b/solution.py
@@ -100,7 +100,14 @@
         .astype(jnp.bfloat16)
     )
     live_slots = (jnp.arange(slots_count, dtype=jnp.int32) < own_count)[None, None, :, None, None]
-    shard_rows = lax.all_gather(grid_panel, "vis", axis=0, tiled=True)
+    world = lax.axis_size("vis")
+    shard_rows = lax.all_to_all(
+        jnp.tile(grid_panel, tuple((world if c == 0 else 1 for c in range(grid_panel.ndim)))),
+        concat_axis=0,
+        axis_name="vis",
+        tiled=True,
+        split_axis=0,
+    )
     rows_here = shard_rows.shape[0]
     split_rows = shard_rows.reshape(rows_here, chan_count, 2, tiles_count, tile_width)
     picked = jnp.einsum(

time: 361 us -> 511 us (1.42); the launches traced: 359 us -> 502 us
  waiting for transfers between devices: 214 us -> 328 us
  starting transfers between devices: 6.25 us -> 26.8 us
  local copies, waits for them, and re-layouts: 70.6 us -> 78.7 us
    all_to_all x0 -> x1, waiting for transfers between devices: none -> 161 us  [per_device(): lax.all_to_all(jnp.tile(grid_panel, tuple((world if c == 0 else 1 for c i...]
    all_gather x1 -> x0, waiting for transfers between devices: 47.8 us -> none  [per_device(): shard_rows = lax.all_gather(grid_panel, 'vis', axis=0, tiled=True)]
    all_to_all x0 -> x1, starting transfers between devices: none -> 9.99 us  [per_device(): lax.all_to_all(jnp.tile(grid_panel, tuple((world if c == 0 else 1 for c i...]
    unnamed x1, starting transfers between devices: 0.22 us -> 10.2 us
    another operation x0 -> x2, local copies, waits for them, and re-layouts: none -> 9.25 us  [the longest x1 8.71 us: per_device(): jnp.tile(grid_panel, tuple((world if c == 0 else 1 for c in range(grid_pa...]
    unnamed x4 -> x3, waiting for transfers between devices: 127 us -> 128 us
  transfers between devices with their start and end apart: 5 -> 5, of which waited for: 5 -> 5; matrix products, arithmetic and copies ran while one was open for 3% -> 2% of each run, Pallas kernels for 0% -> 0%
where the time goes in v1:
time: 511 us; the launch traced here: 502 us
  waiting for transfers between devices  328 us (64%)
  local copies, waits for them, and re-layouts  78.7 us (15%)
  matrix products  46 us (9%)
  starting transfers between devices  26.8 us (5%)
  between operations  16 us (3%)
  other arithmetic  6.21 us (1%)
    all_to_all x1, waiting for transfers between devices, per_device(): lax.all_to_all(jnp.tile(grid_panel, tuple((world if c == 0 else 1 for c i...  161 us
    unnamed x3, waiting for transfers between devices  128 us
    psum x1, waiting for transfers between devices, per_device(): lax.psum(jnp.sum(update * update, axis=1).astype(jnp.bfloat16), 'spec')  36.8 us
    convert_element_type x2, local copies, waits for them, and re-layouts, per_device(): placed.reshape(lax.axis_size('vis') * panel_rows, chan_count, 2, grid_width)  23.6 us
    dot_general x1, matrix products, per_device(): jnp.einsum('omir,rcikn->cokmn', kernel_rows, picked, preferred_element_ty...  15.2 us
    reshape x1, local copies, waits for them, and re-layouts, per_device(): shard_rows.reshape(rows_here, chan_count, 2, tiles_count, tile_width)  14.6 us
    unnamed x15, local copies, waits for them, and re-layouts  14.3 us
  transfers between devices with their start and end apart: 5, of which 5 were waited for; matrix products, arithmetic and copies ran while one was open for 2% of the time, Pallas kernels for 0%

profile of v1, /device:TPU:1, one launch (start us, length us, event | category | flops | bytes accessed | tf_op | source)
XLA Modules:
  0.0 501.7 jit_solution(8489579512657215627)
XLA Ops:
  7.7 1.4 reshape_reshape.3
  15.8 1.1 fusion.19
  19.4 8.7 %tile.4 = bf16[16,8,4,2,4096]{4,3,2,1,0:T(2,128)(2,1)} broadcast(bf16[8,4,2,4096]{3,2,1,0:T(2,128)(2,1)S(1)} %copy.68), dimensions={1,2,3,4} | broadcast | bytes 8912896 | tf_op jit(solution)/shard_map/tile | solution.py:105
  28.1 10.0 %all-to-all-start = ((bf16[128,4,2,4096]{3,2,1,0:T(2,128)(2,1)}), bf16[128,4,2,4096]{3,2,1,0:T(2,128)(2,1)}, u32[]{:S(2)}, u32[]{:S(2)}) async-start(bf16[128,4,2,4096]{3,2,1,0:T(2,128)(2,1)} %bitcast.122), calls=%async_computation | async-start | bytes 16777216 | tf_op jit(solution)/shard_map/all_to_all | solution.py:104
  38.1 10.2 %all-reduce.6.cloned.1.call-start = ((), (), s32[]{:S(2)}) async-start(), calls=%async_computation.2 | async-start | bytes 16777216
  48.3 11.4 %copy.70 = bf16[1,1,4,2,16,256,128]{5,6,4,3,2,1,0:T(8,128)(2,1)} copy(bf16[1,1,4,2,16,256,128]{6,5,4,3,2,1,0:T(8,128)(2,1)} %param.11) | data formatting | bytes 16777216 | tf_op args[4]
  60.5 161.1 %all-to-all-done = bf16[128,4,2,4096]{3,2,1,0:T(2,128)(2,1)} async-done(((bf16[128,4,2,4096]{3,2,1,0:T(2,128)(2,1)}), bf16[128,4,2,4096]{3,2,1,0:T(2,128)(2,1)}, u32[]{:S(2)}, u32[]{:S(2)}) %all-to-all-start) | async-done | bytes 8388640 | tf_op jit(solution)/shard_map/all_to_all | solution.py:104
  221.6 14.6 %reshape.132 = bf16[128,4,2,32,128]{4,3,2,1,0:T(8,128)(2,1)} reshape(bf16[128,4,2,4096]{3,2,1,0:T(2,128)(2,1)} %all-to-all-done) | data formatting | bytes 16777216 | tf_op jit(solution)/shard_map/reshape | solution.py:112
  236.2 4.7 convert_bitcast_fusion.1
  240.9 15.2 %fusion.4 = bf16[4,2,16,256,128,1]{3,4,2,1,0,5:T(8,128)(2,1)} fusion(bf16[1,1,4,2,16,256,128]{5,6,4,3,2,1,0:T(8,128)(2,1)} %copy.70, pred[16]{0:T(512)(128)(4,1)S(1)} %iota_compare_fusion.1, bf16[128,4,2,16,128,1]{4,3,2,1,0,5:T(8,128)(2,1)S(1)} %convert_bitcast_fusion.1, bf16[1,256,2,128]{3,1,2,0:T(8,128)(2,1)S(1)} %get-tuple-element.15, ...), kind=kOutput, calls=%fused_computation.7 | convolution fusion | flops 2164785152 | bytes 21233680 | tf_op jit(solution)/shard_map/omir,rcikn->cokmn/dot_general | solution.py:117
  256.1 7.7 %fusion.5 = bf16[128,4,2,16,128]{0,4,2,3,1:T(8,128)(2,1)} fusion(bf16[4,2,16,256,128,1]{3,4,2,1,0,5:T(8,128)(2,1)} %fusion.4, bf16[1,256,2,128]{3,1,2,0:T(8,128)(2,1)S(1)} %get-tuple-element.15, bf16[1,256,2,128]{3,1,2,0:T(8,128)(2,1)S(1)} %get-tuple-element.14), kind=kOutput, calls=%fused_computation.8 | convolution fusion | flops 2149711872 | bytes 12845056 | tf_op jit(solution)/shard_map/omir,cokmn->rcikn/dot_general | solution.py:124
  263.8 8.0 %copy.73 = bf16[128,4,2,16,128]{4,3,2,1,0:T(8,128)(2,1)} copy(bf16[128,4,2,16,128]{0,4,2,3,1:T(8,128)(2,1)} %fusion.5) | data formatting | bytes 8388608 | tf_op jit(solution)/shard_map/convert_element_type | solution.py:126
  271.8 7.9 %convert_bitcast_fusion = bf16[128,4,2,32,128]{4,3,2,1,0:T(8,128)(2,1)} fusion(bf16[128,4,2,16,128]{4,3,2,1,0:T(8,128)(2,1)} %copy.73, s32[16]{0:T(128)S(1)} %bitcast.131), kind=kOutput, calls=%fused_computation.6 | convolution fusion | flops 138412544 | bytes 12582976 | tf_op jit(solution)/shard_map/rcikn,kt->rcitn/dot_general | solution.py:127
  279.6 12.5 %convert_element_type.120 = bf16[128,4,2,4096]{3,2,1,0:T(2,128)(2,1)} reshape(bf16[128,4,2,32,128]{4,3,2,1,0:T(8,128)(2,1)} %convert_bitcast_fusion) | data formatting | bytes 16777216 | tf_op jit(solution)/shard_map/convert_element_type | solution.py:131
  292.1 11.0 %copy.74 = bf16[128,4,2,4096]{3,1,2,0:T(4,128)(2,1)} copy(bf16[128,4,2,4096]{3,2,1,0:T(2,128)(2,1)} %convert_element_type.120) | data formatting | bytes 16777216 | tf_op jit(solution)/shard_map/convert_element_type | solution.py:131
  304.3 2.6 collective-permute-start
  308.3 128.0 %all-reduce.6.cloned.1.call-done = bf16[128,4,2,4096]{3,1,2,0:T(4,128)(2,1)} async-done(((bf16[128,4,2,4096]{3,1,2,0:T(4,128)(2,1)}), bf16[128,4,2,4096]{3,1,2,0:T(4,128)(2,1)}) %all-reduce.6.cloned.1.call-update) | async-done | bytes 8388624
  436.3 1.2 constant_dynamic-slice_fusion
  438.1 2.3 slice_reduce_fusion.1
  446.1 2.4 multiply_subtract_fusion
  448.6 4.0 collective-permute-start.1
  452.6 1.9 collective-permute-done.1
  454.5 1.3 multiply_reduce_fusion
  455.9 36.8 %all-reduce.4.cloned.1.call-done = bf16[8,4096]{1,0:T(8,128)(2,1)} async-done(((bf16[8,4096]{1,0:T(8,128)(2,1)}), bf16[8,4096]{1,0:T(8,128)(2,1)}) %all-reduce.4.cloned.1.call-update) | async-done | bytes 65552 | tf_op jit(solution)/shard_map/psum | solution.py:158
  (51 shorter events, 19.7 us)
Async XLA Ops:
  28.1 193.5 %all-to-all-start = ((bf16[128,4,2,4096]{3,2,1,0:T(2,128)(2,1)}), bf16[128,4,2,4096]{3,2,1,0:T(2,128)(2,1)}, u32[]{:S(2)}, u32[]{:S(2)}) async-start(bf16[128,4,2,4096]{3,2,1,0:T(2,128)(2,1)} %bitcast.122), calls=%async_computation | async-start | bytes 16777216 | tf_op jit(solution)/shard_map/all_to_all | solution.py:104
  38.1 22.3 %copy-start.2 = (bf16[1,1,2,256,128]{4,3,2,1,0:T(8,128)(2,1)S(1)}, bf16[1,1,2,256,128]{4,3,2,1,0:T(8,128)(2,1)}, u32[]{:S(2)}) copy-start(bf16[1,1,2,256,128]{4,3,2,1,0:T(8,128)(2,1)} %param.10) | copy-start | bytes 393220
  38.1 398.3 %all-reduce.6.cloned.1.call-start = ((), (), s32[]{:S(2)}) async-start(), calls=%async_computation.2 | async-start | bytes 16777216
  60.4 175.7 %copy-start.3 = (s32[1,1,16]{2,1,0:T(1,128)S(1)}, s32[1,1,16]{2,1,0:T(1,128)}, u32[]{:S(2)}) copy-start(s32[1,1,16]{2,1,0:T(1,128)} %param.12) | copy-start | bytes 196
  303.2 1.0 copy-start
  303.2 3.7 copy-start.4
  303.2 189.4 %all-reduce.4.cloned.1.call-start = ((), (), s32[]{:S(2)}) async-start(), calls=%async_computation.1 | async-start | bytes 131072 | tf_op jit(solution)/shard_map/psum | solution.py:158
  304.3 4.0 collective-permute-start
  441.3 51.3 %copy-start.1 = (f32[8,4096]{1,0:T(8,128)S(1)}, f32[8,4096]{1,0:T(8,128)}, u32[]{:S(2)}) copy-start(f32[8,4096]{1,0:T(8,128)} %param.9) | copy-start | bytes 393220
  448.6 5.9 %collective-permute-start.1 = (bf16[3,4,4096]{2,1,0:T(4,128)(2,1)S(1)}, bf16[3,4,4096]{2,1,0:T(4,128)(2,1)S(1)}, u32[]{:S(2)}, u32[]{:S(2)}) collective-permute-start(bf16[3,4,4096]{2,1,0:T(4,128)(2,1)S(1)} %slice.138), channel_id=1, source_target_pairs={{2,0},{4,2},{6,4},{8,6},{10,8},{12,10},{14,12},{16,14},{18,16},{20... | collective-permute-start | bytes 294920 | tf_op jit(solution)/shard_map/ppermute | solution.py:25
Sparse Core Ops, SparseCore 0:
  303.3 132.9 all-reduce.5
  456.0 36.6 all-reduce.3
